TPU v7x, 32 devices: a whole 2x2x4 slice. The times are simulated.
32 devices in a mesh: groups: 2 (over x), tm: 16 (over z, y, core).
Axes of the slice: x: 2, y: 2, z: 4, core: 2. Of those that a mesh axis runs over, the one named last changes fastest.
Arguments:
- observed: float32 [32, 128], P(('groups', 'tm')), parts along dimension 0, may hold values from -6 to 6
- obs_masks: int32 [32, 128], P(('groups', 'tm')), parts along dimension 0, may hold values 0 or 1
- decay_rates: float32 [256], P('groups'), parts along dimension 0, may hold values from 0.05 to 0.5
- noise_var: float32 [256], P('groups'), parts along dimension 0, may hold values from 0.05 to 0.5
- spatial_cov: float32 [256, 128], P('groups'), parts along dimension 0, may hold values from -1 to 4, as said below
Outputs:
- smooth_mean: float32 [32, 256], P(('groups', 'tm')), parts along dimension 0
- smooth_cov: float32 [32, 256, 256], P(('groups', 'tm')), parts along dimension 0
There are 2 independent parts, one for each index of `groups`. A program takes and returns all parts, laid end to end along the dimension named above; each array names one. Nothing has to cross between parts.
Inputs may be any that keep to these rules, and one draw needn't show every extreme that they name: spatial_cov is symmetric, and each diagonal entry is positive and larger than the sum of the magnitudes of the other entries of its row.
All inputs are finite; a program needn't handle non-finite values. No bound on the sum of `obs_masks` on one device may be relied on, other than what follows from the above.
Results may differ from a plain program's by a relative error of at most 0.0003.
Values sent between devices are 32-bit elements; how exact they have to be, the bound alone decides.
No kernel may reach another device: no remote copies, remote signals or barrier semaphores. Data moves between devices by JAX's collectives and lax.ppermute only.
A program may use at most 128 MiB of HBM per device.

v0:
```python
import jax
import jax.numpy as jnp
from jax import lax
from jax.sharding import PartitionSpec as P

HIGHEST = lax.Precision.HIGHEST
JITTER = 0.001


def matmul_hi(left, right):
    return jnp.matmul(left, right, precision=HIGHEST)


def swap_last(matrix):
    return jnp.swapaxes(matrix, -1, -2)


def apply_trans(transit, matrix):
    points = transit.shape[1]
    upper_half = matrix[..., :points, :]
    lower_half = matrix[..., points:, :]
    return jnp.concatenate(
        [
            transit[0][:, None] * upper_half + transit[1][:, None] * lower_half,
            transit[2][:, None] * upper_half + transit[3][:, None] * lower_half,
        ],
        axis=-2,
    )


def build_model(decay_rates, spatial_cov):
    decay_one = jnp.exp(-decay_rates)
    transit = jnp.stack(
        [
            decay_one * (1.0 + decay_rates),
            decay_one * decay_rates,
            -decay_one * decay_rates,
            decay_one * (1.0 - decay_rates),
        ]
    )
    decay_two = jnp.exp(-2.0 * decay_rates)
    var_ff = 1.0 - decay_two * (1.0 + 2.0 * decay_rates + 2.0 * decay_rates * decay_rates)
    cov_fg = 2.0 * decay_rates * decay_rates * decay_two
    var_gg = 1.0 - decay_two * (1.0 - 2.0 * decay_rates + 2.0 * decay_rates * decay_rates)
    fac_ff = jnp.sqrt(var_ff)
    fac_gf = cov_fg / fac_ff
    fac_gg = jnp.sqrt(var_gg - fac_gf * fac_gf)

    def scaled(left, right):
        return left[:, None] * spatial_cov * right[None, :]

    zero_block = jnp.zeros_like(spatial_cov)
    process = jnp.block(
        [
            [scaled(fac_ff, fac_ff), scaled(fac_ff, fac_gf)],
            [scaled(fac_gf, fac_ff), scaled(fac_gf, fac_gf) + scaled(fac_gg, fac_gg)],
        ]
    )
    process = process + JITTER * jnp.eye(2 * spatial_cov.shape[0], dtype=jnp.float32)
    prior = jnp.block([[spatial_cov, zero_block], [zero_block, spatial_cov]])
    return (transit, process, prior)


def predict(transit, process, mean, cov):
    forward_cov = apply_trans(transit, cov)
    cov_pred = apply_trans(transit, swap_last(forward_cov)) + process
    mean_pred = apply_trans(transit, mean[:, None])[:, 0]
    return (mean_pred, cov_pred)


def kalman_update(mean_pred, cov_pred, obs, root):
    points = obs.shape[-1]
    normal = (
        jnp.eye(points, dtype=jnp.float32)
        + root[:, None] * cov_pred[:points, :points] * root[None, :]
    )
    factor = jnp.linalg.cholesky(normal)
    innovation = root * (obs - mean_pred[:points])
    rhs = jnp.concatenate([root[:, None] * cov_pred[:points, :], innovation[:, None]], axis=1)
    half = lax.linalg.triangular_solve(factor, rhs, left_side=True, lower=True)
    gain_half = half[:, :-1]
    cov_new = cov_pred - matmul_hi(swap_last(gain_half), gain_half)
    mean_new = mean_pred + matmul_hi(swap_last(gain_half), half[:, -1])
    return (mean_new, cov_new)


def smoother_elements(means, covs, last_flag, transit, process):
    forward_cov = apply_trans(transit, covs)
    predicted = apply_trans(transit, swap_last(forward_cov)) + process
    factor = jnp.linalg.cholesky(predicted)
    half_solve = lax.linalg.triangular_solve(factor, forward_cov, left_side=True, lower=True)
    gain_t = lax.linalg.triangular_solve(
        factor, half_solve, left_side=True, lower=True, transpose_a=True
    )
    gains = swap_last(gain_t) * (1.0 - last_flag.astype(jnp.float32))[:, None, None]
    forward_mean = apply_trans(transit, means[..., None])
    shift_means = means - matmul_hi(gains, forward_mean)[..., 0]
    shift_covs = covs - matmul_hi(gains, forward_cov)
    return (gains, shift_means, shift_covs)


def smooth_join(lower_el, higher_el):
    gain_a, mean_a, cov_a = lower_el
    gain_b, mean_b, cov_b = higher_el
    return (
        matmul_hi(gain_a, gain_b),
        matmul_hi(gain_a, mean_b[..., None])[..., 0] + mean_a,
        matmul_hi(matmul_hi(gain_a, cov_b), swap_last(gain_a)) + cov_a,
    )


def shards(observed, obs_masks, decay_rates, noise_var, spatial_cov):
    transit, process, prior = build_model(decay_rates, spatial_cov)
    local_steps, points = observed.shape
    width = 2 * points
    position = lax.axis_index("tm")
    tm_count = lax.axis_size("tm")
    total_steps = tm_count * local_steps
    root_local = jnp.sqrt(obs_masks.astype(jnp.float32) / noise_var)
    packed = jnp.stack([observed, root_local], axis=1)
    gathered = lax.all_gather(packed, "tm", tiled=True)
    obs_all = gathered[:, 0]
    root_all = gathered[:, 1]
    mean_first, cov_first = kalman_update(
        jnp.zeros((width,), jnp.float32), prior, obs_all[0], root_all[0]
    )
    last_local = position * local_steps + (local_steps - 1)

    def filter_step(step, mean, cov):
        mean_pred, cov_pred = predict(transit, process, mean, cov)
        obs_now = lax.dynamic_index_in_dim(obs_all, step, keepdims=False)
        root_now = lax.dynamic_index_in_dim(root_all, step, keepdims=False)
        return kalman_update(mean_pred, cov_pred, obs_now, root_now)

    if local_steps == 1:

        def body(step, carry):
            return filter_step(step, carry[0], carry[1])

        mean_last, cov_last = lax.fori_loop(1, last_local + 1, body, (mean_first, cov_first))
        means = mean_last[None]
        covs = cov_last[None]
    else:
        mean_buf = jnp.zeros((local_steps, width), jnp.float32).at[0].set(mean_first)
        cov_buf = jnp.zeros((local_steps, width, width), jnp.float32).at[0].set(cov_first)

        def body(step, carry):
            mean, cov, mean_buf, cov_buf = carry
            mean, cov = filter_step(step, mean, cov)
            slot = step % local_steps
            mean_buf = lax.dynamic_update_index_in_dim(mean_buf, mean, slot, 0)
            cov_buf = lax.dynamic_update_index_in_dim(cov_buf, cov, slot, 0)
            return (mean, cov, mean_buf, cov_buf)

        _, _, means, covs = lax.fori_loop(
            1, last_local + 1, body, (mean_first, cov_first, mean_buf, cov_buf)
        )
    global_step = position * local_steps + jnp.arange(local_steps)
    last_flag = global_step == total_steps - 1
    if local_steps == 1:

        def compute_elements(operand):
            return smoother_elements(operand[0], operand[1], last_flag, transit, process)

        def final_elements(operand):
            return (jnp.zeros_like(operand[1]), operand[0], operand[1])

        smooth = lax.cond(position == tm_count - 1, final_elements, compute_elements, (means, covs))
    else:
        smooth = smoother_elements(means, covs, last_flag, transit, process)
    if local_steps > 1:
        last_el = jax.tree.map(lambda leaf: leaf[-1], smooth)
        front_els = jax.tree.map(lambda leaf: leaf[:-1], smooth)

        def backward(running, element):
            joined = smooth_join(element, running)
            return (joined, joined)

        _, head_els = lax.scan(backward, last_el, front_els, reverse=True)
        suffixes = jax.tree.map(
            lambda head_leaf, last_leaf: jnp.concatenate([head_leaf, last_leaf[None]], axis=0),
            head_els,
            last_el,
        )
        block_total = jax.tree.map(lambda leaf: leaf[0], suffixes)
    else:
        block_total = jax.tree.map(lambda leaf: leaf[0], smooth)
    running = block_total
    shift = 1
    while shift < tm_count:
        pairs = [(source, source - shift) for source in range(shift, tm_count)]
        received = lax.ppermute(running, "tm", pairs)
        running = smooth_join(running, received)
        shift *= 2
    if local_steps == 1:
        return (running[1][None], running[2][None])
    pairs = [(source, source - 1) for source in range(1, tm_count)]
    after_mine = lax.ppermute(running, "tm", pairs)
    gains, shift_means, shift_covs = suffixes
    smooth_mean = matmul_hi(gains, after_mine[1][:, None])[..., 0] + shift_means
    smooth_cov = matmul_hi(matmul_hi(gains, after_mine[2]), swap_last(gains)) + shift_covs
    return (smooth_mean, smooth_cov)


def solution(mesh):
    placed = (
        P(("groups", "tm"), None),
        P(("groups", "tm"), None),
        P("groups"),
        P("groups"),
        P("groups", None),
    )
    return jax.shard_map(
        shards,
        mesh=mesh,
        in_specs=placed,
        out_specs=(P(("groups", "tm"), None), P(("groups", "tm"), None, None)),
        check_vma=False,
    )
```

profile of v0, /device:TPU:1, one launch (start us, length us, event | category | flops | bytes accessed | tf_op | source)
XLA Modules:
  0.0 498.3 jit_solution(2744481612989866936)
XLA Ops:
  2.0 23.1 %all_gather.3 = f32[16,2,128]{2,1,0:T(2,128)S(1)} all-gather(f32[1,2,128]{2,1,0:T(2,128)S(1)} %pad_maximum_fusion.3), channel_id=1, replica_groups=mesh['groups'=2,'tm'=16] {'tm'}, dimensions={0}, use_global_device_ids=true | all-gather | bytes 17408 | tf_op jit(solution)/shard_map/all_gather | solution.py:121
  25.7 11.7 %custom-call.32 = f32[128,128]{1,0:T(8,128)S(1)} custom-call(f32[128,128]{1,0:T(8,128)S(1)} %fusion.49), custom_call_target="Cholesky" | custom-call | tf_op jit(solution)/shard_map/jit(cholesky)/cholesky/custom-call.1 | solution.py:77
  38.8 9.8 %custom-call.33 = f32[1,128,128]{1,2,0:T(8,128)S(1)} custom-call(f32[1,128,128]{2,1,0:T(8,128)S(1)} %fusion.47), custom_call_target="InvertDiagBlocksLowerTriangular" | custom-call | tf_op jit(solution)/shard_map/triangular_solve/custom-call.0 | solution.py:80
  49.9 24.9 %while.14 = (s32[]{:T(128)}, f32[256]{0:T(256)S(1)}, f32[256,256]{0,1:T(8,128)S(1)}, s32[]{:T(128)}, f32[128]{0:T(128)S(1)}, /*index=5*/f32[128]{0:T(128)S(1)}, ...) while((s32[]{:T(128)}, f32[256]{0:T(256)S(1)}, ...), condition=%wide.region_3.6_spmd, body=%wide.region_2.5_spmd.sunk | while | flops 152618752 | bytes 5461689 | solution.py:140
  51.0 11.7 %custom-call.37 = f32[128,128]{1,0:T(8,128)S(1)} custom-call(f32[128,128]{1,0:T(8,128)S(1)} %fusion.129), custom_call_target="Cholesky" | custom-call | tf_op jit(solution)/shard_map/while/body/jit(cholesky)/cholesky/custom-call.1 | solution.py:77
  64.0 9.8 %custom-call.38 = f32[1,128,128]{1,2,0:T(8,128)S(1)} custom-call(f32[1,128,128]{2,1,0:T(8,128)S(1)} %fusion.130), custom_call_target="InvertDiagBlocksLowerTriangular" | custom-call | tf_op jit(solution)/shard_map/while/body/triangular_solve/custom-call.0 | solution.py:80
  74.9 63.7 %conditional.1 = (f32[1,256]{1,0:T(1,128)S(1)}, f32[256,256]{0,1:T(8,128)S(1)}, f32[1,256,256]{2,1,0:T(8,128)S(1)}) conditional(s32[]{:T(128)} %convert_element_type.18, (f32[128]{0:T(128)S(1)}, f32[1,256,256]{1,2,0:T(8,128)S(1)}, f32[128]{0:T(128)S(1)}, f32[128]{0:T(128)S(1)}, f32[128]{0:T(128)S(1)}, /*index=5*/f32[256,256]{0,1:T(8,128)S(1)}, ...), branch_computations={%region_4.11_spmd, %region_9.12_spmd} | conditional | flops 556025344 | bytes 11482373 | solution.py:168
  76.0 11.7 %custom-call.24 = f32[1,128,128]{2,1,0:T(8,128)S(1)} custom-call(f32[1,128,128]{2,1,0:T(8,128)S(1)} %cholesky.48), custom_call_target="Cholesky" | custom-call | tf_op jit(solution)/shard_map/cond/branch_0_fun/jit(cholesky)/cholesky | solution.py:90
  87.7 9.8 %custom-call.25 = f32[1,1,128,128]{2,3,1,0:T(8,128)S(1)} custom-call(f32[1,1,128,128]{3,2,1,0:T(8,128)S(1)} %get-tuple-element.221), custom_call_target="InvertDiagBlocksLowerTriangular" | custom-call | tf_op jit(solution)/shard_map/cond/branch_0_fun/jit(cholesky)/cholesky | solution.py:90
  98.0 11.7 %custom-call.26 = f32[1,128,128]{2,1,0:T(8,128)S(1)} custom-call(f32[1,128,128]{2,1,0:T(8,128)S(1)} %fusion.20), custom_call_target="Cholesky" | custom-call | tf_op jit(solution)/shard_map/cond/branch_0_fun/jit(cholesky)/cholesky | solution.py:90
  111.8 4.0 while.13
  115.7 19.7 %custom-call.27 = f32[1,2,128,128]{2,3,1,0:T(8,128)S(1)} custom-call(f32[1,2,128,128]{3,2,1,0:T(8,128)S(1)} %bitcast.262), custom_call_target="InvertDiagBlocksLowerTriangular" | custom-call | tf_op jit(solution)/shard_map/cond/branch_0_fun/triangular_solve | solution.py:92
  138.6 1.9 collective-permute-start.7
  140.5 1.9 collective-permute-start.3
  142.4 1.9 collective-permute-start
  144.3 22.5 %collective-permute-done.3 = f32[256]{0:T(256)S(1)} collective-permute-done((f32[256]{0:T(256)S(1)}, f32[256]{0:T(256)S(1)}, u32[]{:S(2)}, u32[]{:S(2)}) %collective-permute-start.3) | collective-permute-done | bytes 1056 | tf_op jit(solution)/shard_map/ppermute | solution.py:192
  172.6 48.7 %collective-permute-done.4 = f32[256]{0:T(256)S(1)} collective-permute-done((f32[256]{0:T(256)S(1)}, f32[256]{0:T(256)S(1)}, u32[]{:S(2)}, u32[]{:S(2)}) %collective-permute-start.4) | collective-permute-done | bytes 1056 | tf_op jit(solution)/shard_map/ppermute | solution.py:192
  221.6 1.3 collective-permute-start.5
  222.9 4.1 collective-permute-done.8
  231.5 89.9 %collective-permute-done.5 = f32[256]{0:T(256)S(1)} collective-permute-done((f32[256]{0:T(256)S(1)}, f32[256]{0:T(256)S(1)}, u32[]{:S(2)}, u32[]{:S(2)}) %collective-permute-start.5) | collective-permute-done | bytes 1056 | tf_op jit(solution)/shard_map/ppermute | solution.py:192
  321.7 1.3 collective-permute-start.6
  323.1 7.4 %collective-permute-done.9 = f32[256,256]{1,0:T(8,128)S(1)} collective-permute-done((f32[256,256]{1,0:T(8,128)S(1)}, f32[256,256]{1,0:T(8,128)S(1)}, u32[]{:S(2)}, u32[]{:S(2)}) %collective-permute-start.9) | collective-permute-done | bytes 262176 | tf_op jit(solution)/shard_map/ppermute | solution.py:192
  333.7 145.0 %collective-permute-done.6 = f32[256]{0:T(256)S(1)} collective-permute-done((f32[256]{0:T(256)S(1)}, f32[256]{0:T(256)S(1)}, u32[]{:S(2)}, u32[]{:S(2)}) %collective-permute-start.6) | collective-permute-done | bytes 1056 | tf_op jit(solution)/shard_map/ppermute | solution.py:192
  479.6 17.0 %collective-permute-done.10 = f32[256,256]{1,0:T(8,128)S(1)} collective-permute-done((f32[256,256]{1,0:T(8,128)S(1)}, f32[256,256]{1,0:T(8,128)S(1)}, u32[]{:S(2)}, u32[]{:S(2)}) %collective-permute-start.10) | collective-permute-done | bytes 262176 | tf_op jit(solution)/shard_map/ppermute | solution.py:192
  (115 shorter events, 32.1 us)
Async XLA Ops:
  0.6 0.7 copy-start.3
  0.6 0.7 copy-start.4
  1.3 0.7 copy-start.1
  2.0 23.2 %copy-start.2 = (f32[128]{0:T(128)S(1)}, f32[128]{0:T(128)}, u32[]{:S(2)}) copy-start(f32[128]{0:T(128)} %param.14) | copy-start | bytes 1540
  2.0 23.3 %copy-start = (f32[128,128]{1,0:T(8,128)S(1)}, f32[128,128]{1,0:T(8,128)}, u32[]{:S(2)}) copy-start(f32[128,128]{1,0:T(8,128)} %param.16) | copy-start | bytes 196612
  138.6 29.8 %collective-permute-start.7 = (f32[256,256]{1,0:T(8,128)S(1)}, f32[256,256]{1,0:T(8,128)S(1)}, u32[]{:S(2)}, u32[]{:S(2)}) collective-permute-start(f32[256,256]{1,0:T(8,128)S(1)} %bitcast.242), channel_id=1, source_target_pairs={{1,0},{2,1},{3,2},{4,3},{5,4},{6,5},{7,6},{8,7},{9,8},{10,9},{11,1... | collective-permute-start | bytes 786440 | tf_op jit(solution)/shard_map/ppermute | solution.py:192
  140.5 26.3 %collective-permute-start.3 = (f32[256]{0:T(256)S(1)}, f32[256]{0:T(256)S(1)}, u32[]{:S(2)}, u32[]{:S(2)}) collective-permute-start(f32[256]{0:T(256)S(1)} %bitcast.255), channel_id=1, source_target_pairs={{1,0},{2,1},{3,2},{4,3},{5,4},{6,5},{7,6},{8,7},{9,8},{10,9},{11,1... | collective-permute-start | bytes 3080 | tf_op jit(solution)/shard_map/ppermute | solution.py:192
  142.4 28.2 %collective-permute-start = (f32[256,256]{0,1:T(8,128)S(1)}, f32[256,256]{0,1:T(8,128)S(1)}, u32[]{:S(2)}, u32[]{:S(2)}) collective-permute-start(f32[256,256]{0,1:T(8,128)S(1)} %get-tuple-element.136), channel_id=1, source_target_pairs={{1,0},{2,1},{3,2},{4,3},{5,4},{6,5},{7,6},{8,7},{9,8},{10,9},{11,1... | collective-permute-start | bytes 786440 | tf_op jit(solution)/shard_map/ppermute | solution.py:192
  167.0 54.3 %collective-permute-start.4 = (f32[256]{0:T(256)S(1)}, f32[256]{0:T(256)S(1)}, u32[]{:S(2)}, u32[]{:S(2)}) collective-permute-start(f32[256]{0:T(256)S(1)} %add.183), channel_id=1, source_target_pairs={{2,0},{3,1},{4,2},{5,3},{6,4},{7,5},{8,6},{9,7},{10,8},{11,9},{12,... | collective-permute-start | bytes 3080 | tf_op jit(solution)/shard_map/ppermute | solution.py:192
  169.4 57.7 %collective-permute-start.8 = (f32[256,256]{1,0:T(8,128)S(1)}, f32[256,256]{1,0:T(8,128)S(1)}, u32[]{:S(2)}, u32[]{:S(2)}) collective-permute-start(f32[256,256]{1,0:T(8,128)S(1)} %convolution_add_fusion.3), channel_id=1, source_target_pairs={{2,0},{3,1},{4,2},{5,3},{6,4},{7,5},{8,6},{9,7},{10,8},{11,9},{12,... | collective-permute-start | bytes 786440 | tf_op jit(solution)/shard_map/ppermute | solution.py:192
  171.3 58.6 %collective-permute-start.1 = (f32[256,256]{1,0:T(8,128)S(1)}, f32[256,256]{1,0:T(8,128)S(1)}, u32[]{:S(2)}, u32[]{:S(2)}) collective-permute-start(f32[256,256]{1,0:T(8,128)S(1)} %fusion.59), channel_id=1, source_target_pairs={{2,0},{3,1},{4,2},{5,3},{6,4},{7,5},{8,6},{9,7},{10,8},{11,9},{12,... | collective-permute-start | bytes 786440 | tf_op jit(solution)/shard_map/ppermute | solution.py:192
  221.6 99.9 %collective-permute-start.5 = (f32[256]{0:T(256)S(1)}, f32[256]{0:T(256)S(1)}, u32[]{:S(2)}, u32[]{:S(2)}) collective-permute-start(f32[256]{0:T(256)S(1)} %add.184), channel_id=1, source_target_pairs={{4,0},{5,1},{6,2},{7,3},{8,4},{9,5},{10,6},{11,7},{12,8},{13,9},{1... | collective-permute-start | bytes 3080 | tf_op jit(solution)/shard_map/ppermute | solution.py:192
  227.8 102.6 %collective-permute-start.9 = (f32[256,256]{1,0:T(8,128)S(1)}, f32[256,256]{1,0:T(8,128)S(1)}, u32[]{:S(2)}, u32[]{:S(2)}) collective-permute-start(f32[256,256]{1,0:T(8,128)S(1)} %convolution_add_fusion.2), channel_id=1, source_target_pairs={{4,0},{5,1},{6,2},{7,3},{8,4},{9,5},{10,6},{11,7},{12,8},{13,9},{1... | collective-permute-start | bytes 786440 | tf_op jit(solution)/shard_map/ppermute | solution.py:192
  230.2 103.1 %collective-permute-start.2 = (f32[256,256]{1,0:T(8,128)S(1)}, f32[256,256]{1,0:T(8,128)S(1)}, u32[]{:S(2)}, u32[]{:S(2)}) collective-permute-start(f32[256,256]{1,0:T(8,128)S(1)} %fusion.60), channel_id=1, source_target_pairs={{4,0},{5,1},{6,2},{7,3},{8,4},{9,5},{10,6},{11,7},{12,8},{13,9},{1... | collective-permute-start | bytes 786440 | tf_op jit(solution)/shard_map/ppermute | solution.py:192
  321.7 156.9 %collective-permute-start.6 = (f32[256]{0:T(256)S(1)}, f32[256]{0:T(256)S(1)}, u32[]{:S(2)}, u32[]{:S(2)}) collective-permute-start(f32[256]{0:T(256)S(1)} %add.185), channel_id=1, source_target_pairs={{8,0},{9,1},{10,2},{11,3},{12,4},{13,5},{14,6},{15,7},{24,16},{25,... | collective-permute-start | bytes 3080 | tf_op jit(solution)/shard_map/ppermute | solution.py:192
  331.3 165.3 %collective-permute-start.10 = (f32[256,256]{1,0:T(8,128)S(1)}, f32[256,256]{1,0:T(8,128)S(1)}, u32[]{:S(2)}, u32[]{:S(2)}) collective-permute-start(f32[256,256]{1,0:T(8,128)S(1)} %convolution_add_fusion.1), channel_id=1, source_target_pairs={{8,0},{9,1},{10,2},{11,3},{12,4},{13,5},{14,6},{15,7},{24,16},{25,... | collective-permute-start | bytes 786440 | tf_op jit(solution)/shard_map/ppermute | solution.py:192
where the time goes:
time: 505 us; the launch traced here: 498 us
  waiting for transfers between devices  336 us (67%)
  other arithmetic  100 us (20%)
  blocking collectives  23.1 us (5%)
  starting transfers between devices  16.2 us (3%)
  matrix products  12.2 us (2%)
  local copies, waits for them, and re-layouts  6.42 us (1%)
    ppermute x11, waiting for transfers between devices, shards(): received = lax.ppermute(running, 'tm', pairs)  336 us
    another operation x6, other arithmetic, smoother_elements(): factor = jnp.linalg.cholesky(predicted)  34 us
    another operation x6, other arithmetic, kalman_update(): factor = jnp.linalg.cholesky(normal)  24.9 us
    all_gather x1, blocking collectives, shards(): gathered = lax.all_gather(packed, 'tm', tiled=True)  23.1 us
    another operation x4, other arithmetic, kalman_update(): half = lax.linalg.triangular_solve(factor, rhs, left_side=True, lower=True)  20.9 us
    another operation x3, other arithmetic, smoother_elements(): lax.linalg.triangular_solve(factor, half_solve, left_side=True, lower=Tru...  19.7 us
    ppermute x11, starting transfers between devices, shards(): received = lax.ppermute(running, 'tm', pairs)  16.2 us
  transfers between devices with their start and end apart: 11, of which 9 were waited for; matrix products, arithmetic and copies ran while one was open for 1% of the time, Pallas kernels for 0%

commit v1 on v0

--- a/solution.py
+++ b/solution.py
@@ -1,3 +1,4 @@
+import functools
 import jax
 import jax.numpy as jnp
 from jax import lax
@@ -5,6 +6,25 @@
 
 HIGHEST = lax.Precision.HIGHEST
 JITTER = 0.001
+
+
+def make_column(mine_x, comm_axis):
+    arr_now = lax.axis_size(comm_axis)
+    next_value, t_next, q_next = (arr_now, lax.axis_index(comm_axis), mine_x.shape[0])
+    near, t1 = (mine_x, 1)
+    while t1 < next_value:
+        g_now = lax.ppermute(
+            near,
+            axis_name=comm_axis,
+            perm=list(map(lambda j0: (j0, (j0 - t1) % next_value), range(next_value))),
+        )
+        near = jnp.concatenate([near, g_now], axis=0)
+        t1 = 2 * t1
+    side_arr = jnp.roll(near, shift=t_next * q_next, axis=0)
+    return side_arr
+
+
+set_points = functools.partial(make_column, comm_axis="tm")
 
 
 def matmul_hi(left, right):
@@ -118,7 +138,7 @@
     total_steps = tm_count * local_steps
     root_local = jnp.sqrt(obs_masks.astype(jnp.float32) / noise_var)
     packed = jnp.stack([observed, root_local], axis=1)
-    gathered = lax.all_gather(packed, "tm", tiled=True)
+    gathered = set_points(packed)
     obs_all = gathered[:, 0]
     root_all = gathered[:, 1]
     mean_first, cov_first = kalman_update(

time: 505 us -> 506 us (level)
  blocking collectives: 23.1 us -> 0 us
  waiting for transfers between devices: 336 us -> 350 us
  starting transfers between devices: 16.2 us -> 23.9 us
    all_gather x1 -> x0, blocking collectives: 23.1 us -> none  [shards(): gathered = lax.all_gather(packed, 'tm', tiled=True)]
    ppermute x0 -> x4, waiting for transfers between devices: none -> 8.26 us  [make_column(): lax.ppermute(near, axis_name=comm_axis, perm=list(map(lambda j0: (j0, (j0...]
    ppermute x0 -> x4, starting transfers between devices: none -> 7.66 us  [make_column(): lax.ppermute(near, axis_name=comm_axis, perm=list(map(lambda j0: (j0, (j0...]
    ppermute x11, waiting for transfers between devices: 336 us -> 342 us  [shards(): received = lax.ppermute(running, 'tm', pairs)]
  transfers between devices with their start and end apart: 11 -> 15, of which waited for: 9 -> 13; matrix products, arithmetic and copies ran while one was open for 1% -> 1% of each run, Pallas kernels for 0% -> 0%
where the time goes in v1:
time: 506 us; the launch traced here: 499 us
  waiting for transfers between devices  350 us (69%)
  other arithmetic  101 us (20%)
  starting transfers between devices  23.9 us (5%)
  matrix products  12.2 us (2%)
  local copies, waits for them, and re-layouts  8.22 us (2%)
    ppermute x11, waiting for transfers between devices, shards(): received = lax.ppermute(running, 'tm', pairs)  342 us
    another operation x6, other arithmetic, smoother_elements(): factor = jnp.linalg.cholesky(predicted)  34 us
    another operation x6, other arithmetic, kalman_update(): factor = jnp.linalg.cholesky(normal)  24.8 us
    another operation x4, other arithmetic, kalman_update(): half = lax.linalg.triangular_solve(factor, rhs, left_side=True, lower=True)  20.8 us
    another operation x3, other arithmetic, smoother_elements(): lax.linalg.triangular_solve(factor, half_solve, left_side=True, lower=Tru...  19.7 us
    ppermute x11, starting transfers between devices, shards(): received = lax.ppermute(running, 'tm', pairs)  16.2 us
  transfers between devices with their start and end apart: 15, of which 13 were waited for; matrix products, arithmetic and copies ran while one was open for 1% of the time, Pallas kernels for 0%

profile of v1, /device:TPU:1, one launch (start us, length us, event | category | flops | bytes accessed | tf_op | source)
XLA Modules:
  0.0 499.2 jit_solution(3551064235634140143)
XLA Ops:
  3.7 2.2 collective-permute-done
  5.9 7.0 %collective-permute-start.1 = (f32[2,2,128]{2,1,0:T(2,128)S(1)}, f32[2,2,128]{2,1,0:T(2,128)S(1)}, u32[]{:S(2)}, u32[]{:S(2)}) collective-permute-start(f32[2,2,128]{2,1,0:T(2,128)S(1)} %pad_maximum_fusion.5), channel_id=1, source_target_pairs={{0,14},{1,15},{2,0},{3,1},{4,2},{5,3},{6,4},{7,5},{8,6},{9,7},{10,... | collective-permute-start | bytes 6152 | tf_op jit(solution)/shard_map/ppermute | solution.py:16
  16.2 3.5 collective-permute-done.3
  20.8 11.7 %custom-call.32 = f32[128,128]{1,0:T(8,128)S(1)} custom-call(f32[128,128]{1,0:T(8,128)S(1)} %fusion.49), custom_call_target="Cholesky" | custom-call | tf_op jit(solution)/shard_map/jit(cholesky)/cholesky/custom-call.1 | solution.py:97
  33.8 9.8 %custom-call.33 = f32[1,128,128]{1,2,0:T(8,128)S(1)} custom-call(f32[1,128,128]{2,1,0:T(8,128)S(1)} %fusion.47), custom_call_target="InvertDiagBlocksLowerTriangular" | custom-call | tf_op jit(solution)/shard_map/triangular_solve/custom-call.0 | solution.py:100
  44.9 24.8 %while.14 = (s32[]{:T(128)}, f32[256]{0:T(256)S(1)}, f32[256,256]{0,1:T(8,128)S(1)}, s32[]{:T(128)}, f32[128]{0:T(128)S(1)}, /*index=5*/f32[128]{0:T(128)S(1)}, ...) while((s32[]{:T(128)}, f32[256]{0:T(256)S(1)}, ...), condition=%wide.region_3.6_spmd, body=%wide.region_2.5_spmd.sunk | while | flops 152618752 | bytes 5461689 | solution.py:160
  45.9 11.7 %custom-call.39 = f32[128,128]{1,0:T(8,128)S(1)} custom-call(f32[128,128]{1,0:T(8,128)S(1)} %fusion.130), custom_call_target="Cholesky" | custom-call | tf_op jit(solution)/shard_map/while/body/jit(cholesky)/cholesky/custom-call.1 | solution.py:97
  58.9 9.8 %custom-call.40 = f32[1,128,128]{1,2,0:T(8,128)S(1)} custom-call(f32[1,128,128]{2,1,0:T(8,128)S(1)} %fusion.131), custom_call_target="InvertDiagBlocksLowerTriangular" | custom-call | tf_op jit(solution)/shard_map/while/body/triangular_solve/custom-call.0 | solution.py:100
  69.7 64.1 %conditional.1 = (f32[1,256]{1,0:T(1,128)S(1)}, f32[256,256]{0,1:T(8,128)S(1)}, f32[1,256,256]{2,1,0:T(8,128)S(1)}) conditional(s32[]{:T(128)} %convert_element_type.18, (f32[128]{0:T(128)S(1)}, f32[1,256,256]{1,2,0:T(8,128)S(1)}, f32[128]{0:T(128)S(1)}, f32[128]{0:T(128)S(1)}, f32[128]{0:T(128)S(1)}, /*index=5*/f32[256,256]{0,1:T(8,128)S(1)}, ...), branch_computations={%region_4.11_spmd, %region_9.12_spmd} | conditional | flops 556025344 | bytes 11482373 | solution.py:188
  70.8 11.7 %custom-call.24 = f32[1,128,128]{2,1,0:T(8,128)S(1)} custom-call(f32[1,128,128]{2,1,0:T(8,128)S(1)} %cholesky.48), custom_call_target="Cholesky" | custom-call | tf_op jit(solution)/shard_map/cond/branch_0_fun/jit(cholesky)/cholesky | solution.py:110
  82.6 9.8 %custom-call.25 = f32[1,1,128,128]{2,3,1,0:T(8,128)S(1)} custom-call(f32[1,1,128,128]{3,2,1,0:T(8,128)S(1)} %get-tuple-element.207), custom_call_target="InvertDiagBlocksLowerTriangular" | custom-call | tf_op jit(solution)/shard_map/cond/branch_0_fun/jit(cholesky)/cholesky | solution.py:110
  92.9 11.7 %custom-call.26 = f32[1,128,128]{2,1,0:T(8,128)S(1)} custom-call(f32[1,128,128]{2,1,0:T(8,128)S(1)} %fusion.20), custom_call_target="Cholesky" | custom-call | tf_op jit(solution)/shard_map/cond/branch_0_fun/jit(cholesky)/cholesky | solution.py:110
  106.8 4.2 while.13
  111.0 19.7 %custom-call.27 = f32[1,2,128,128]{2,3,1,0:T(8,128)S(1)} custom-call(f32[1,2,128,128]{3,2,1,0:T(8,128)S(1)} %bitcast.266), custom_call_target="InvertDiagBlocksLowerTriangular" | custom-call | tf_op jit(solution)/shard_map/cond/branch_0_fun/triangular_solve | solution.py:112
  133.8 1.9 collective-permute-start.11
  135.7 1.9 collective-permute-start.7
  137.7 1.9 collective-permute-start.4
  139.6 27.3 %collective-permute-done.7 = f32[256]{0:T(256)S(1)} collective-permute-done((f32[256]{0:T(256)S(1)}, f32[256]{0:T(256)S(1)}, u32[]{:S(2)}, u32[]{:S(2)}) %collective-permute-start.7) | collective-permute-done | bytes 1056 | tf_op jit(solution)/shard_map/ppermute | solution.py:212
  172.6 46.0 %collective-permute-done.8 = f32[256]{0:T(256)S(1)} collective-permute-done((f32[256]{0:T(256)S(1)}, f32[256]{0:T(256)S(1)}, u32[]{:S(2)}, u32[]{:S(2)}) %collective-permute-start.8) | collective-permute-done | bytes 1056 | tf_op jit(solution)/shard_map/ppermute | solution.py:212
  220.3 4.1 collective-permute-done.12
  228.9 91.4 %collective-permute-done.9 = f32[256]{0:T(256)S(1)} collective-permute-done((f32[256]{0:T(256)S(1)}, f32[256]{0:T(256)S(1)}, u32[]{:S(2)}, u32[]{:S(2)}) %collective-permute-start.9) | collective-permute-done | bytes 1056 | tf_op jit(solution)/shard_map/ppermute | solution.py:212
  322.0 7.4 %collective-permute-done.13 = f32[256,256]{1,0:T(8,128)S(1)} collective-permute-done((f32[256,256]{1,0:T(8,128)S(1)}, f32[256,256]{1,0:T(8,128)S(1)}, u32[]{:S(2)}, u32[]{:S(2)}) %collective-permute-start.13) | collective-permute-done | bytes 262176 | tf_op jit(solution)/shard_map/ppermute | solution.py:212
  332.6 147.0 %collective-permute-done.10 = f32[256]{0:T(256)S(1)} collective-permute-done((f32[256]{0:T(256)S(1)}, f32[256]{0:T(256)S(1)}, u32[]{:S(2)}, u32[]{:S(2)}) %collective-permute-start.10) | collective-permute-done | bytes 1056 | tf_op jit(solution)/shard_map/ppermute | solution.py:212
  480.5 17.0 %collective-permute-done.14 = f32[256,256]{1,0:T(8,128)S(1)} collective-permute-done((f32[256,256]{1,0:T(8,128)S(1)}, f32[256,256]{1,0:T(8,128)S(1)}, u32[]{:S(2)}, u32[]{:S(2)}) %collective-permute-start.14) | collective-permute-done | bytes 262176 | tf_op jit(solution)/shard_map/ppermute | solution.py:212
  (130 shorter events, 40.5 us)
Async XLA Ops:
  1.3 0.7 copy-start.1
  2.0 3.9 collective-permute-start
  2.0 0.7 copy-start.2
  5.9 7.7 %collective-permute-start.1 = (f32[2,2,128]{2,1,0:T(2,128)S(1)}, f32[2,2,128]{2,1,0:T(2,128)S(1)}, u32[]{:S(2)}, u32[]{:S(2)}) collective-permute-start(f32[2,2,128]{2,1,0:T(2,128)S(1)} %pad_maximum_fusion.5), channel_id=1, source_target_pairs={{0,14},{1,15},{2,0},{3,1},{4,2},{5,3},{6,4},{7,5},{8,6},{9,7},{10,... | collective-permute-start | bytes 6152 | tf_op jit(solution)/shard_map/ppermute | solution.py:16
  13.6 2.5 collective-permute-start.2
  16.1 3.5 collective-permute-start.3
  19.7 0.8 copy-start
  133.8 34.6 %collective-permute-start.11 = (f32[256,256]{1,0:T(8,128)S(1)}, f32[256,256]{1,0:T(8,128)S(1)}, u32[]{:S(2)}, u32[]{:S(2)}) collective-permute-start(f32[256,256]{1,0:T(8,128)S(1)} %bitcast.242), channel_id=1, source_target_pairs={{1,0},{2,1},{3,2},{4,3},{5,4},{6,5},{7,6},{8,7},{9,8},{10,9},{11,1... | collective-permute-start | bytes 786440 | tf_op jit(solution)/shard_map/ppermute | solution.py:212
  135.7 31.2 %collective-permute-start.7 = (f32[256]{0:T(256)S(1)}, f32[256]{0:T(256)S(1)}, u32[]{:S(2)}, u32[]{:S(2)}) collective-permute-start(f32[256]{0:T(256)S(1)} %bitcast.260), channel_id=1, source_target_pairs={{1,0},{2,1},{3,2},{4,3},{5,4},{6,5},{7,6},{8,7},{9,8},{10,9},{11,1... | collective-permute-start | bytes 3080 | tf_op jit(solution)/shard_map/ppermute | solution.py:212
  137.7 33.1 %collective-permute-start.4 = (f32[256,256]{0,1:T(8,128)S(1)}, f32[256,256]{0,1:T(8,128)S(1)}, u32[]{:S(2)}, u32[]{:S(2)}) collective-permute-start(f32[256,256]{0,1:T(8,128)S(1)} %get-tuple-element.136), channel_id=1, source_target_pairs={{1,0},{2,1},{3,2},{4,3},{5,4},{6,5},{7,6},{8,7},{9,8},{10,9},{11,1... | collective-permute-start | bytes 786440 | tf_op jit(solution)/shard_map/ppermute | solution.py:212
  167.1 51.6 %collective-permute-start.8 = (f32[256]{0:T(256)S(1)}, f32[256]{0:T(256)S(1)}, u32[]{:S(2)}, u32[]{:S(2)}) collective-permute-start(f32[256]{0:T(256)S(1)} %add.195), channel_id=1, source_target_pairs={{2,0},{3,1},{4,2},{5,3},{6,4},{7,5},{8,6},{9,7},{10,8},{11,9},{12,... | collective-permute-start | bytes 3080 | tf_op jit(solution)/shard_map/ppermute | solution.py:212
  169.4 55.0 %collective-permute-start.12 = (f32[256,256]{1,0:T(8,128)S(1)}, f32[256,256]{1,0:T(8,128)S(1)}, u32[]{:S(2)}, u32[]{:S(2)}) collective-permute-start(f32[256,256]{1,0:T(8,128)S(1)} %convolution_add_fusion.3), channel_id=1, source_target_pairs={{2,0},{3,1},{4,2},{5,3},{6,4},{7,5},{8,6},{9,7},{10,8},{11,9},{12,... | collective-permute-start | bytes 786440 | tf_op jit(solution)/shard_map/ppermute | solution.py:212
  171.3 55.9 %collective-permute-start.5 = (f32[256,256]{1,0:T(8,128)S(1)}, f32[256,256]{1,0:T(8,128)S(1)}, u32[]{:S(2)}, u32[]{:S(2)}) collective-permute-start(f32[256,256]{1,0:T(8,128)S(1)} %fusion.60), channel_id=1, source_target_pairs={{2,0},{3,1},{4,2},{5,3},{6,4},{7,5},{8,6},{9,7},{10,8},{11,9},{12,... | collective-permute-start | bytes 786440 | tf_op jit(solution)/shard_map/ppermute | solution.py:212
  219.0 101.4 %collective-permute-start.9 = (f32[256]{0:T(256)S(1)}, f32[256]{0:T(256)S(1)}, u32[]{:S(2)}, u32[]{:S(2)}) collective-permute-start(f32[256]{0:T(256)S(1)} %add.196), channel_id=1, source_target_pairs={{4,0},{5,1},{6,2},{7,3},{8,4},{9,5},{10,6},{11,7},{12,8},{13,9},{1... | collective-permute-start | bytes 3080 | tf_op jit(solution)/shard_map/ppermute | solution.py:212
  225.2 104.1 %collective-permute-start.13 = (f32[256,256]{1,0:T(8,128)S(1)}, f32[256,256]{1,0:T(8,128)S(1)}, u32[]{:S(2)}, u32[]{:S(2)}) collective-permute-start(f32[256,256]{1,0:T(8,128)S(1)} %convolution_add_fusion.2), channel_id=1, source_target_pairs={{4,0},{5,1},{6,2},{7,3},{8,4},{9,5},{10,6},{11,7},{12,8},{13,9},{1... | collective-permute-start | bytes 786440 | tf_op jit(solution)/shard_map/ppermute | solution.py:212
  227.6 104.6 %collective-permute-start.6 = (f32[256,256]{1,0:T(8,128)S(1)}, f32[256,256]{1,0:T(8,128)S(1)}, u32[]{:S(2)}, u32[]{:S(2)}) collective-permute-start(f32[256,256]{1,0:T(8,128)S(1)} %fusion.61), channel_id=1, source_target_pairs={{4,0},{5,1},{6,2},{7,3},{8,4},{9,5},{10,6},{11,7},{12,8},{13,9},{1... | collective-permute-start | bytes 786440 | tf_op jit(solution)/shard_map/ppermute | solution.py:212
  320.6 159.0 %collective-permute-start.10 = (f32[256]{0:T(256)S(1)}, f32[256]{0:T(256)S(1)}, u32[]{:S(2)}, u32[]{:S(2)}) collective-permute-start(f32[256]{0:T(256)S(1)} %add.197), channel_id=1, source_target_pairs={{8,0},{9,1},{10,2},{11,3},{12,4},{13,5},{14,6},{15,7},{24,16},{25,... | collective-permute-start | bytes 3080 | tf_op jit(solution)/shard_map/ppermute | solution.py:212
  330.2 167.3 %collective-permute-start.14 = (f32[256,256]{1,0:T(8,128)S(1)}, f32[256,256]{1,0:T(8,128)S(1)}, u32[]{:S(2)}, u32[]{:S(2)}) collective-permute-start(f32[256,256]{1,0:T(8,128)S(1)} %convolution_add_fusion.1), channel_id=1, source_target_pairs={{8,0},{9,1},{10,2},{11,3},{12,4},{13,5},{14,6},{15,7},{24,16},{25,... | collective-permute-start | bytes 786440 | tf_op jit(solution)/shard_map/ppermute | solution.py:212
